TPU v7x, 256 devices: a whole 4x4x8 slice. The times are simulated.
256 devices in a mesh: row: 16 (over z_hi, x, core), col: 16 (over y, z_lo).
Axes of the slice: x: 4, y: 4, z: 8 (z_hi: 2, z_lo: 4; z = z_hi * 4 + z_lo), core: 2. Of those that a mesh axis runs over, the one named last changes fastest.
Arguments:
- points: float32 [64, 32768], P(None, ('row', 'col')), may hold values from -24 to 24, as said below
- embedding: float32 [2, 32768], P(None, ('row', 'col')), may hold values from -8 to 8
- precision: float32 [32768], P(('row', 'col')), may hold values from 0.05 to 2
Outputs:
- force: float32 [2, 32768], P(None, ('row', 'col'))
- calibrated: float32 [32768], P(('row', 'col'))
Inputs may be any that keep to these rules, and one draw needn't show every extreme that they name: `points`: each point's coordinates are normal values times a positive scale of that point.
All inputs are finite; a program needn't handle non-finite values.
Results may differ from a plain program's by a relative error of at most 0.0003.
Values sent between devices are 32-bit elements; how exact they have to be, the bound alone decides.
No kernel may reach another device: no remote copies, remote signals or barrier semaphores. Data moves between devices by JAX's collectives and lax.ppermute only.
A program may use at most 64 MiB of HBM per device.

v0:
```python
import math
import jax
import jax.numpy as jnp
from jax import lax
from jax.sharding import PartitionSpec as P

PERP = 30


def newton_update(zsum, first, second, start_prec):
    entropy = jnp.log(zsum) + start_prec * first / zsum
    spread = second / zsum - (first / zsum) ** 2
    factor = jnp.clip(
        (entropy - math.log(PERP)) / jnp.maximum(start_prec * start_prec * spread, 1.0), -2.0, 2.0
    )
    return start_prec * jnp.exp(factor)


def col_stage(values):
    count = lax.axis_size("col")
    held = values
    shift = 1
    while shift < count:
        pairs = [(i, (i + shift) % count) for i in range(count)]
        held = jnp.concatenate([held, lax.ppermute(held, "col", pairs)], axis=1)
        shift *= 2
    return held


def spread_all(values):
    return lax.all_gather(col_stage(values), "row", axis=1, tiled=True)


def body(points, embedding, precision):
    per_dev = points.shape[1]
    width = points.shape[0]
    axes = ("row", "col")
    own_start = lax.axis_index("row") * lax.axis_size("col") * per_dev
    own_coords = points
    own_map = embedding
    own_sq = jnp.sum(own_coords * own_coords, axis=0)
    packed = jnp.concatenate([points, embedding, own_sq[None, :]], axis=0)
    every = spread_all(packed)
    total = every.shape[1]
    all_coords = every[:width]
    all_map = every[width : width + 2]
    all_sq = every[width + 2]
    inner = lax.dot_general(
        own_coords,
        all_coords,
        (((0,), (0,)), ((), ())),
        precision=lax.Precision.HIGHEST,
        preferred_element_type=jnp.float32,
    )
    distance = jnp.maximum(own_sq[:, None] + all_sq[None, :] - 2.0 * inner, 0.0)
    col_ids = jnp.arange(total, dtype=jnp.int32)[None, :]
    row_ids = (own_start + jnp.arange(per_dev, dtype=jnp.int32))[:, None]
    itself = row_ids == col_ids
    nearest = jnp.min(jnp.where(itself, jnp.inf, distance), axis=1)
    shifted = distance - nearest[:, None]
    expo = jnp.where(itself, 0.0, jnp.exp(-precision[:, None] * shifted))
    zsum = jnp.sum(expo, axis=1)
    first = jnp.sum(expo * shifted, axis=1)
    second = jnp.sum(expo * shifted * shifted, axis=1)
    calib = newton_update(zsum, first, second, precision)
    norm = jnp.sum(jnp.where(itself, 0.0, jnp.exp(-calib[:, None] * shifted)), axis=1)
    delta_a = own_map[0][:, None] - all_map[0][None, :]
    delta_b = own_map[1][:, None] - all_map[1][None, :]
    kernel = jnp.where(itself, 0.0, 1.0 / (1.0 + delta_a * delta_a + delta_b * delta_b))
    kernel_part = jnp.sum(kernel)
    qslot = jnp.where(jnp.arange(per_dev) == 0, kernel_part, 0.0)
    stats = jnp.stack([calib, nearest, 1.0 / norm, qslot])
    all_stats = spread_all(stats)
    calib_cols = all_stats[0]
    nearest_cols = all_stats[1]
    inv_norm_cols = all_stats[2]
    qsum = jnp.sum(all_stats[3])
    cond_rows = jnp.exp(-calib[:, None] * shifted) * (1.0 / norm)[:, None]
    cond_cols = (
        jnp.exp(-calib_cols[None, :] * (distance - nearest_cols[None, :])) * inv_norm_cols[None, :]
    )
    affinity = jnp.where(itself, 0.0, 0.5 * (cond_rows + cond_cols))
    coef = (affinity - total * kernel / qsum) * kernel
    force = jnp.stack([jnp.sum(coef * delta_a, axis=1), jnp.sum(coef * delta_b, axis=1)])
    return (force, calib)


def solution(mesh):
    in_specs = (P(None, ("row", "col")), P(None, ("row", "col")), P(("row", "col")))
    out_specs = (P(None, ("row", "col")), P(("row", "col")))
    return jax.shard_map(body, mesh=mesh, in_specs=in_specs, out_specs=out_specs, check_vma=False)
```

profile of v0, /device:TPU:1, one launch (start us, length us, event | category | flops | bytes accessed | tf_op | source)
XLA Modules:
  0.0 310.4 jit_solution(2971438880049326950)
XLA Ops:
  7.2 0.8 multiply_reduce_fusion.1
  8.0 0.8 pad_maximum_fusion.3
  8.8 2.5 collective-permute-start
  11.2 6.5 %collective-permute-done = f32[67,128]{1,0:T(8,128)S(1)} collective-permute-done((f32[67,128]{1,0:T(8,128)S(1)}, f32[67,128]{1,0:T(8,128)S(1)}, u32[]{:S(2)}, u32[]{:S(2)}) %collective-permute-start) | collective-permute-done | bytes 34336 | tf_op jit(solution)/shard_map/ppermute | solution.py:25
  17.7 0.8 pad_maximum_fusion.2
  18.6 6.2 %collective-permute-done.1 = f32[67,256]{1,0:T(8,128)S(1)} collective-permute-done((f32[67,256]{1,0:T(8,128)S(1)}, f32[67,256]{1,0:T(8,128)S(1)}, u32[]{:S(2)}, u32[]{:S(2)}) %collective-permute-start.1) | collective-permute-done | bytes 68640 | tf_op jit(solution)/shard_map/ppermute | solution.py:25
  24.8 0.8 pad_maximum_fusion.1
  25.5 0.1 collective-permute-start.2
  25.6 5.2 %collective-permute-done.2 = f32[67,512]{1,0:T(8,128)S(1)} collective-permute-done((f32[67,512]{1,0:T(8,128)S(1)}, f32[67,512]{1,0:T(8,128)S(1)}, u32[]{:S(2)}, u32[]{:S(2)}) %collective-permute-start.2) | collective-permute-done | bytes 137248 | tf_op jit(solution)/shard_map/ppermute | solution.py:25
  30.8 0.8 pad_maximum_fusion
  31.6 0.1 collective-permute-start.3
  31.8 7.0 %collective-permute-done.3 = f32[67,1024]{1,0:T(8,128)S(1)} collective-permute-done((f32[67,1024]{1,0:T(8,128)S(1)}, f32[67,1024]{1,0:T(8,128)S(1)}, u32[]{:S(2)}, u32[]{:S(2)}) %collective-permute-start.3) | collective-permute-done | bytes 274464 | tf_op jit(solution)/shard_map/ppermute | solution.py:25
  38.8 0.8 copy-done
  39.6 0.7 neg.12
  40.3 0.8 slice_bitcast_fusion.1
  41.1 118.7 %all-gather.2.cloned.1.call-done = f32[67,32768]{1,0:T(8,128)} async-done(((f32[67,2048]{1,0:T(8,128)}), f32[67,32768]{1,0:T(8,128)}) %all-gather.2.cloned.1.call-update) | async-done | bytes 8781840 | tf_op jit(solution)/shard_map/all_gather | solution.py:31
  159.8 2.6 fusion.15
  162.4 40.7 %select_reduce_fusion.1 = (f32[128]{0:T(128)S(1)}, f32[128,32768]{0,1:T(8,128)S(1)}) fusion(s32[128]{0:T(128)S(1)} %iota_add_fusion, f32[64,128]{1,0:T(8,128)} %param.3, f32[67,32768]{1,0:T(8,128)} %all-gather.2.cloned.1.call-done, f32[32768]{0:T(1024)S(1)} %bitcast.31, f32[128]{0:T(128)S(1)} %multiply_reduce_fusion.1), kind=kOutput, calls=%fused_computation.22 | convolution fusion | flops 3250585600 | bytes 25331200 | tf_op jit(solution)/shard_map/dot_general | solution.py:48
  203.2 6.6 %multiply_reduce_fusion = (f32[128]{0:T(128)S(1)}, f32[128]{0:T(128)S(1)}, f32[128]{0:T(128)S(1)}) fusion(f32[128,32768]{0,1:T(8,128)S(1)} %get-tuple-element.25, f32[128]{0:T(128)S(1)} %get-tuple-element.24, f32[128]{0:T(128)S(1)} %neg.12, s32[128]{0:T(128)S(1)} %iota_add_fusion), kind=kLoop, calls=%fused_computation.17 | loop fusion | flops 37748352 | bytes 16780288 | tf_op jit(solution)/shard_map/reduce_sum | solution.py:64
  209.8 17.8 %select_reduce_fusion = (f32[128]{0:T(128)S(1)}, f32[]{:T(128)}) fusion(f32[128,32768]{0,1:T(8,128)S(1)} %get-tuple-element.25, f32[128]{0:T(128)S(1)} %get-tuple-element.9, f32[128]{0:T(128)S(1)} %get-tuple-element.24, s32[128]{0:T(128)S(1)} %iota_add_fusion, f32[32768]{0:T(1024)S(1)} %bitcast.26, f32[128]{0:T(128)S(1)} %get-tuple-element.23, ...), kind=kLoop, calls=%fused_computation.15 | loop fusion | flops 58720128 | bytes 17042436 | tf_op jit(solution)/shard_map/reduce_sum | solution.py:66
  227.5 0.6 compare_select_fusion
  228.2 0.3 collective-permute-start.4
  228.5 6.1 %collective-permute-done.4 = f32[4,128]{1,0:T(4,128)S(1)} collective-permute-done((f32[4,128]{1,0:T(4,128)S(1)}, f32[4,128]{1,0:T(4,128)S(1)}, u32[]{:S(2)}, u32[]{:S(2)}) %collective-permute-start.4) | collective-permute-done | bytes 2080 | tf_op jit(solution)/shard_map/ppermute | solution.py:25
  234.7 0.1 collective-permute-start.5
  234.8 5.4 %collective-permute-done.5 = f32[4,256]{1,0:T(4,128)S(1)} collective-permute-done((f32[4,256]{1,0:T(4,128)S(1)}, f32[4,256]{1,0:T(4,128)S(1)}, u32[]{:S(2)}, u32[]{:S(2)}) %collective-permute-start.5) | collective-permute-done | bytes 4128 | tf_op jit(solution)/shard_map/ppermute | solution.py:25
  240.3 3.7 %collective-permute-done.6 = f32[4,512]{1,0:T(4,128)S(1)} collective-permute-done((f32[4,512]{1,0:T(4,128)S(1)}, f32[4,512]{1,0:T(4,128)S(1)}, u32[]{:S(2)}, u32[]{:S(2)}) %collective-permute-start.6) | collective-permute-done | bytes 8224 | tf_op jit(solution)/shard_map/ppermute | solution.py:25
  244.0 0.1 collective-permute-start.7
  244.1 4.1 %collective-permute-done.7 = f32[4,1024]{1,0:T(4,128)S(1)} collective-permute-done((f32[4,1024]{1,0:T(4,128)S(1)}, f32[4,1024]{1,0:T(4,128)S(1)}, u32[]{:S(2)}, u32[]{:S(2)}) %collective-permute-start.7) | collective-permute-done | bytes 16416 | tf_op jit(solution)/shard_map/ppermute | solution.py:25
  248.2 30.1 %all_gather.7 = f32[4,32768]{1,0:T(4,128)S(1)} all-gather(f32[4,2048]{1,0:T(4,128)S(1)} %constant_dynamic-update-slice_fusion.5), channel_id=1, replica_groups=mesh['row'=16,'col'=16] {'row'}, dimensions={1}, use_global_device_ids=true | all-gather | bytes 557056 | tf_op jit(solution)/shard_map/all_gather | solution.py:31
  278.3 1.0 slice_negate_fusion
  279.3 23.7 %fusion.7 = (f32[128]{0:T(128)S(1)}, f32[128]{0:T(128)S(1)}) fusion(f32[32768]{0:T(1024)S(1)} %bitcast.25, f32[128]{0:T(128)S(1)} %get-tuple-element.22, f32[32768]{0:T(1024)S(1)} %bitcast.27, f32[128]{0:T(128)S(1)} %get-tuple-element.23, f32[]{:T(128)} %get-tuple-element.15, f32[32768]{0:T(1024)S(1)} %bitcast.29, f32[128,32768]{0,1:T(8,128)S(1)} %get-tuple-element.25, ...), kind=kLoop, calls=%fused_computation.12 | loop fusion | flops 109051648 | bytes 17436676 | tf_op jit(solution)/shard_map/reduce_sum | solution.py:84
  303.0 0.6 pad_maximum_fusion.8
  (25 shorter events, 0.3 us)
Async XLA Ops:
  7.2 152.6 %all-gather.2.cloned.1.call-start = ((), (), s32[]{:S(2)}) async-start(), calls=%async_computation | async-start | bytes 10027008 | tf_op jit(solution)/shard_map/all_gather | solution.py:31
  8.8 9.0 %collective-permute-start = (f32[67,128]{1,0:T(8,128)S(1)}, f32[67,128]{1,0:T(8,128)S(1)}, u32[]{:S(2)}, u32[]{:S(2)}) collective-permute-start(f32[67,128]{1,0:T(8,128)S(1)} %get-tuple-element.18), channel_id=1, source_target_pairs={{0,1},{1,2},{2,3},{3,4},{4,5},{5,6},{6,7},{7,8},{8,9},{9,10},{10,1... | collective-permute-start | bytes 102920 | tf_op jit(solution)/shard_map/ppermute | solution.py:25
  18.5 6.2 %collective-permute-start.1 = (f32[67,256]{1,0:T(8,128)S(1)}, f32[67,256]{1,0:T(8,128)S(1)}, u32[]{:S(2)}, u32[]{:S(2)}) collective-permute-start(f32[67,256]{1,0:T(8,128)S(1)} %pad_maximum_fusion.2), channel_id=1, source_target_pairs={{0,2},{1,3},{2,4},{3,5},{4,6},{5,7},{6,8},{7,9},{8,10},{9,11},{10,... | collective-permute-start | bytes 205832 | tf_op jit(solution)/shard_map/ppermute | solution.py:25
  25.5 5.3 %collective-permute-start.2 = (f32[67,512]{1,0:T(8,128)S(1)}, f32[67,512]{1,0:T(8,128)S(1)}, u32[]{:S(2)}, u32[]{:S(2)}) collective-permute-start(f32[67,512]{1,0:T(8,128)S(1)} %pad_maximum_fusion.1), channel_id=1, source_target_pairs={{0,4},{1,5},{2,6},{3,7},{4,8},{5,9},{6,10},{7,11},{8,12},{9,13},{1... | collective-permute-start | bytes 411656 | tf_op jit(solution)/shard_map/ppermute | solution.py:25
  31.6 7.2 %collective-permute-start.3 = (f32[67,1024]{1,0:T(8,128)S(1)}, f32[67,1024]{1,0:T(8,128)S(1)}, u32[]{:S(2)}, u32[]{:S(2)}) collective-permute-start(f32[67,1024]{1,0:T(8,128)S(1)} %pad_maximum_fusion), channel_id=1, source_target_pairs={{0,8},{1,9},{2,10},{3,11},{4,12},{5,13},{6,14},{7,15},{8,0},{9,1},... | collective-permute-start | bytes 823304 | tf_op jit(solution)/shard_map/ppermute | solution.py:25
  38.8 0.8 copy-start
  203.2 6.6 %copy-start.2 = (f32[128]{0:T(128)S(1)}, f32[128]{0:T(128)}, u32[]{:S(2)}) copy-start(f32[128]{0:T(128)} %param.5) | copy-start | bytes 1540
  209.8 93.2 %copy-start.1 = (f32[128]{0:T(128)}, f32[128]{0:T(128)S(1)}, u32[]{:S(2)}) copy-start(f32[128]{0:T(128)S(1)} %get-tuple-element.10) | copy-start | bytes 1540
  228.2 6.4 %collective-permute-start.4 = (f32[4,128]{1,0:T(4,128)S(1)}, f32[4,128]{1,0:T(4,128)S(1)}, u32[]{:S(2)}, u32[]{:S(2)}) collective-permute-start(f32[4,128]{1,0:T(4,128)S(1)} %get-tuple-element.20), channel_id=1, source_target_pairs={{0,1},{1,2},{2,3},{3,4},{4,5},{5,6},{6,7},{7,8},{8,9},{9,10},{10,1... | collective-permute-start | bytes 6152 | tf_op jit(solution)/shard_map/ppermute | solution.py:25
  234.7 5.5 %collective-permute-start.5 = (f32[4,256]{1,0:T(4,128)S(1)}, f32[4,256]{1,0:T(4,128)S(1)}, u32[]{:S(2)}, u32[]{:S(2)}) collective-permute-start(f32[4,256]{1,0:T(4,128)S(1)} %pad_maximum_fusion.6), channel_id=1, source_target_pairs={{0,2},{1,3},{2,4},{3,5},{4,6},{5,7},{6,8},{7,9},{8,10},{9,11},{10,... | collective-permute-start | bytes 12296 | tf_op jit(solution)/shard_map/ppermute | solution.py:25
  240.2 3.8 %collective-permute-start.6 = (f32[4,512]{1,0:T(4,128)S(1)}, f32[4,512]{1,0:T(4,128)S(1)}, u32[]{:S(2)}, u32[]{:S(2)}) collective-permute-start(f32[4,512]{1,0:T(4,128)S(1)} %pad_maximum_fusion.5), channel_id=1, source_target_pairs={{0,4},{1,5},{2,6},{3,7},{4,8},{5,9},{6,10},{7,11},{8,12},{9,13},{1... | collective-permute-start | bytes 24584 | tf_op jit(solution)/shard_map/ppermute | solution.py:25
  244.0 4.2 %collective-permute-start.7 = (f32[4,1024]{1,0:T(4,128)S(1)}, f32[4,1024]{1,0:T(4,128)S(1)}, u32[]{:S(2)}, u32[]{:S(2)}) collective-permute-start(f32[4,1024]{1,0:T(4,128)S(1)} %pad_maximum_fusion.4), channel_id=1, source_target_pairs={{0,8},{1,9},{2,10},{3,11},{4,12},{5,13},{6,14},{7,15},{8,0},{9,1},... | collective-permute-start | bytes 49160 | tf_op jit(solution)/shard_map/ppermute | solution.py:25
Sparse Core Ops, SparseCore 0:
  39.8 119.9 all-gather.1
where the time goes:
time: 311 us; the launch traced here: 310 us
  waiting for transfers between devices  163 us (52%)
  other arithmetic  54.9 us (18%)
  matrix products  40.7 us (13%)
  blocking collectives  30.1 us (10%)
  between operations  14.2 us (5%)
  local copies, waits for them, and re-layouts  4.27 us (1%)
  starting transfers between devices  3.27 us (1%)
    all_gather x1, waiting for transfers between devices, spread_all(): return lax.all_gather(col_stage(values), 'row', axis=1, tiled=True)  119 us
    ppermute x8, waiting for transfers between devices, col_stage(): held = jnp.concatenate([held, lax.ppermute(held, 'col', pairs)], axis=1)  44.2 us
    dot_general x1, matrix products, body(): lax.dot_general(own_coords, all_coords, (((0,), (0,)), ((), ())), precisi...  40.7 us
    all_gather x1, blocking collectives, spread_all(): return lax.all_gather(col_stage(values), 'row', axis=1, tiled=True)  30.1 us
    reduce_sum x1, other arithmetic, body(): jnp.sum(coef * delta_a, axis=1)  23.7 us
    reduce_sum x1, other arithmetic, body(): jnp.sum(jnp.where(itself, 0.0, jnp.exp(-calib[:, None] * shifted)), axis=1)  17.8 us
    reduce_sum x1, other arithmetic, body(): second = jnp.sum(expo * shifted * shifted, axis=1)  6.56 us
  transfers between devices with their start and end apart: 9, of which 9 were waited for; matrix products, arithmetic and copies ran while one was open for 0% of the time, Pallas kernels for 0%

commit v1 on v0

--- a/solution.py
+++ b/solution.py
@@ -28,7 +28,9 @@
 
 
 def spread_all(values):
-    return lax.all_gather(col_stage(values), "row", axis=1, tiled=True)
+    return jnp.concatenate(
+        lax.all_to_all(jnp.stack([col_stage(values)] * lax.axis_size("row")), "row", 0, 0), axis=1
+    )
 
 
 def body(points, embedding, precision):

time: 311 us -> 456 us (1.47)
  waiting for transfers between devices: 163 us -> 293 us
  starting transfers between devices: 3.27 us -> 49.3 us
  blocking collectives: 30.1 us -> 0 us
  between operations: 14.2 us -> 0.87 us
  local copies, waits for them, and re-layouts: 4.27 us -> 13.4 us
    all_to_all x0 -> x2, waiting for transfers between devices: none -> 253 us  [spread_all(): lax.all_to_all(jnp.stack([col_stage(values)] * lax.axis_size('row')), 'ro...]
    all_gather x1 -> x0, waiting for transfers between devices: 119 us -> none  [spread_all(): return lax.all_gather(col_stage(values), 'row', axis=1, tiled=True)]
    all_to_all x0 -> x2, starting transfers between devices: none -> 33.5 us  [spread_all(): lax.all_to_all(jnp.stack([col_stage(values)] * lax.axis_size('row')), 'ro...]
    all_gather x1 -> x0, blocking collectives: 30.1 us -> none  [spread_all(): return lax.all_gather(col_stage(values), 'row', axis=1, tiled=True)]
    ppermute x8, starting transfers between devices: 3.23 us -> 15.8 us  [col_stage(): held = jnp.concatenate([held, lax.ppermute(held, 'col', pairs)], axis=1)]
    another operation x0 -> x2, local copies, waits for them, and re-layouts: none -> 5.73 us  [spread_all(): jnp.stack([col_stage(values)] * lax.axis_size('row'))]
    ppermute x8, waiting for transfers between devices: 44.2 us -> 39.5 us  [col_stage(): held = jnp.concatenate([held, lax.ppermute(held, 'col', pairs)], axis=1)]
  transfers between devices with their start and end apart: 9 -> 10, of which waited for: 9 -> 10; matrix products, arithmetic and copies ran while one was open for 0% -> 0% of each run, Pallas kernels for 0% -> 0%
where the time goes in v1:
time: 456 us; the launch traced here: 452 us
  waiting for transfers between devices  293 us (64%)
  other arithmetic  56.9 us (12%)
  starting transfers between devices  49.3 us (11%)
  matrix products  39.2 us (9%)
  local copies, waits for them, and re-layouts  13.4 us (3%)
    all_to_all x2, waiting for transfers between devices, spread_all(): lax.all_to_all(jnp.stack([col_stage(values)] * lax.axis_size('row')), 'ro...  253 us
    ppermute x8, waiting for transfers between devices, col_stage(): held = jnp.concatenate([held, lax.ppermute(held, 'col', pairs)], axis=1)  39.5 us
    dot_general x1, matrix products, body(): lax.dot_general(own_coords, all_coords, (((0,), (0,)), ((), ())), precisi...  39.2 us
    all_to_all x2, starting transfers between devices, spread_all(): lax.all_to_all(jnp.stack([col_stage(values)] * lax.axis_size('row')), 'ro...  33.5 us
    reduce_sum x1, other arithmetic, body(): jnp.sum(coef * delta_a, axis=1)  26.3 us
    reduce_sum x1, other arithmetic, body(): jnp.sum(jnp.where(itself, 0.0, jnp.exp(-calib[:, None] * shifted)), axis=1)  17.8 us
    ppermute x8, starting transfers between devices, col_stage(): held = jnp.concatenate([held, lax.ppermute(held, 'col', pairs)], axis=1)  15.8 us
  transfers between devices with their start and end apart: 10, of which 10 were waited for; matrix products, arithmetic and copies ran while one was open for 0% of the time, Pallas kernels for 0%

profile of v1, /device:TPU:1, one launch (start us, length us, event | category | flops | bytes accessed | tf_op | source)
XLA Modules:
  0.0 452.5 jit_solution(18343177491798030475)
XLA Ops:
  0.7 0.8 multiply_reduce_fusion.1
  1.4 0.8 pad_maximum_fusion.3
  2.2 2.5 collective-permute-start
  4.7 6.5 %collective-permute-done = f32[67,128]{1,0:T(8,128)S(1)} collective-permute-done((f32[67,128]{1,0:T(8,128)S(1)}, f32[67,128]{1,0:T(8,128)S(1)}, u32[]{:S(2)}, u32[]{:S(2)}) %collective-permute-start) | collective-permute-done | bytes 34336 | tf_op jit(solution)/shard_map/ppermute | solution.py:25
  11.2 0.8 pad_maximum_fusion.2
  12.0 6.2 %collective-permute-done.1 = f32[67,256]{1,0:T(8,128)S(1)} collective-permute-done((f32[67,256]{1,0:T(8,128)S(1)}, f32[67,256]{1,0:T(8,128)S(1)}, u32[]{:S(2)}, u32[]{:S(2)}) %collective-permute-start.1) | collective-permute-done | bytes 68640 | tf_op jit(solution)/shard_map/ppermute | solution.py:25
  18.2 0.8 pad_maximum_fusion.1
  19.1 5.2 %collective-permute-done.2 = f32[67,512]{1,0:T(8,128)S(1)} collective-permute-done((f32[67,512]{1,0:T(8,128)S(1)}, f32[67,512]{1,0:T(8,128)S(1)}, u32[]{:S(2)}, u32[]{:S(2)}) %collective-permute-start.2) | collective-permute-done | bytes 137248 | tf_op jit(solution)/shard_map/ppermute | solution.py:25
  24.3 0.8 pad_maximum_fusion
  25.2 7.0 %collective-permute-done.3 = f32[67,1024]{1,0:T(8,128)S(1)} collective-permute-done((f32[67,1024]{1,0:T(8,128)S(1)}, f32[67,1024]{1,0:T(8,128)S(1)}, u32[]{:S(2)}, u32[]{:S(2)}) %collective-permute-start.3) | collective-permute-done | bytes 274464 | tf_op jit(solution)/shard_map/ppermute | solution.py:25
  32.3 4.8 %stack.16 = f32[16,67,2048]{2,1,0:T(8,128)} broadcast(f32[67,2048]{1,0:T(8,128)S(1)} %constant_dynamic-update-slice_fusion), dimensions={1,2} | broadcast | bytes 9330688 | tf_op jit(solution)/shard_map/stack | solution.py:32
  37.1 14.8 %all-to-all-start = ((f32[16,67,2048]{2,1,0:T(8,128)}), f32[16,67,2048]{2,1,0:T(8,128)}, u32[]{:S(2)}, u32[]{:S(2)}) async-start(f32[16,67,2048]{2,1,0:T(8,128)} %stack.16), calls=%async_computation | async-start | bytes 18874368 | tf_op jit(solution)/shard_map/all_to_all | solution.py:32
  51.9 238.7 %all-to-all-done = f32[16,67,2048]{2,1,0:T(8,128)} async-done(((f32[16,67,2048]{2,1,0:T(8,128)}), f32[16,67,2048]{2,1,0:T(8,128)}, u32[]{:S(2)}, u32[]{:S(2)}) %all-to-all-start) | async-done | bytes 8781856 | tf_op jit(solution)/shard_map/all_to_all | solution.py:32
  290.7 2.5 fusion.14
  293.1 4.0 slice_bitcast_fusion
  297.1 1.1 copy.10
  298.2 39.2 %select_reduce_fusion.1 = (f32[128]{0:T(128)S(1)}, f32[128,32768]{0,1:T(8,128)S(1)}) fusion(s32[128]{0:T(128)S(1)} %iota_add_fusion, f32[64,32768]{1,0:T(8,128)S(1)} %bitcast.30, f32[64,128]{1,0:T(8,128)S(1)} %copy-done.1, f32[32768]{0:T(1024)S(1)} %bitcast.39, f32[128]{0:T(128)S(1)} %multiply_reduce_fusion.1), kind=kOutput, calls=%fused_computation.22 | convolution fusion | flops 3250585600 | bytes 25331200 | tf_op jit(solution)/shard_map/dot_general | solution.py:50
  337.5 6.6 %multiply_reduce_fusion = (f32[128]{0:T(128)S(1)}, f32[128]{0:T(128)S(1)}, f32[128]{0:T(128)S(1)}) fusion(f32[128,32768]{0,1:T(8,128)S(1)} %get-tuple-element.25, f32[128]{0:T(128)S(1)} %get-tuple-element.24, f32[128]{0:T(128)S(1)} %neg.20, s32[128]{0:T(128)S(1)} %iota_add_fusion), kind=kLoop, calls=%fused_computation.17 | loop fusion | flops 37748352 | bytes 16780288 | tf_op jit(solution)/shard_map/reduce_sum | solution.py:66
  344.1 17.8 %select_reduce_fusion = (f32[128]{0:T(128)S(1)}, f32[]{:T(128)}) fusion(f32[128,32768]{0,1:T(8,128)S(1)} %get-tuple-element.25, f32[128]{0:T(128)S(1)} %get-tuple-element.9, f32[128]{0:T(128)S(1)} %get-tuple-element.24, s32[128]{0:T(128)S(1)} %iota_add_fusion, f32[32768]{0:T(1024)S(1)} %bitcast.34, f32[128]{0:T(128)S(1)} %get-tuple-element.23, ...), kind=kLoop, calls=%fused_computation.15 | loop fusion | flops 58720128 | bytes 17042436 | tf_op jit(solution)/shard_map/reduce_sum | solution.py:68
  361.9 0.6 compare_select_fusion
  362.6 6.3 %collective-permute-done.4 = f32[4,128]{1,0:T(4,128)S(1)} collective-permute-done((f32[4,128]{1,0:T(4,128)S(1)}, f32[4,128]{1,0:T(4,128)S(1)}, u32[]{:S(2)}, u32[]{:S(2)}) %collective-permute-start.4) | collective-permute-done | bytes 2080 | tf_op jit(solution)/shard_map/ppermute | solution.py:25
  369.1 5.4 %collective-permute-done.5 = f32[4,256]{1,0:T(4,128)S(1)} collective-permute-done((f32[4,256]{1,0:T(4,128)S(1)}, f32[4,256]{1,0:T(4,128)S(1)}, u32[]{:S(2)}, u32[]{:S(2)}) %collective-permute-start.5) | collective-permute-done | bytes 4128 | tf_op jit(solution)/shard_map/ppermute | solution.py:25
  374.5 10.8 %collective-permute-start.6 = (f32[4,512]{1,0:T(4,128)S(1)}, f32[4,512]{1,0:T(4,128)S(1)}, u32[]{:S(2)}, u32[]{:S(2)}) collective-permute-start(f32[4,512]{1,0:T(4,128)S(1)} %pad_maximum_fusion.5), channel_id=1, source_target_pairs={{0,4},{1,5},{2,6},{3,7},{4,8},{5,9},{6,10},{7,11},{8,12},{9,13},{1... | collective-permute-start | bytes 24584 | tf_op jit(solution)/shard_map/ppermute | solution.py:25
  385.4 0.8 collective-permute-done.6
  386.2 2.1 collective-permute-start.7
  388.3 2.0 collective-permute-done.7
  390.4 0.9 stack.20
  391.2 18.7 %all-to-all-start.1 = ((f32[16,4,2048]{2,1,0:T(4,128)}), f32[16,4,2048]{2,1,0:T(4,128)S(1)}, u32[]{:S(2)}, u32[]{:S(2)}) async-start(f32[16,4,2048]{2,1,0:T(4,128)} %stack.20), calls=%async_computation.1 | async-start | bytes 1048576 | tf_op jit(solution)/shard_map/all_to_all | solution.py:32
  410.0 14.6 %all-to-all-done.1 = f32[16,4,2048]{2,1,0:T(4,128)S(1)} async-done(((f32[16,4,2048]{2,1,0:T(4,128)}), f32[16,4,2048]{2,1,0:T(4,128)S(1)}, u32[]{:S(2)}, u32[]{:S(2)}) %all-to-all-start.1) | async-done | bytes 524320 | tf_op jit(solution)/shard_map/all_to_all | solution.py:32
  424.6 1.0 slice_negate_fusion
  425.6 26.3 %fusion.7 = (f32[128]{0:T(128)S(1)}, f32[128]{0:T(128)S(1)}) fusion(f32[32768]{0:T(1024)S(1)} %bitcast.33, f32[128]{0:T(128)S(1)} %get-tuple-element.22, f32[32768]{0:T(1024)S(1)} %bitcast.35, f32[128]{0:T(128)S(1)} %get-tuple-element.23, f32[]{:T(128)} %get-tuple-element.15, f32[32768]{0:T(1024)S(1)} %bitcast.37, f32[128,32768]{0,1:T(8,128)} %copy-done, ...), kind=kLoop, calls=%fused_computation.12 | loop fusion | flops 109051648 | bytes 17436676 | tf_op jit(solution)/shard_map/reduce_sum | solution.py:86
  451.9 0.6 pad_maximum_fusion.8
  (33 shorter events, 0.6 us)
Async XLA Ops:
  0.6 51.3 %copy-start.2 = (f32[2,128]{1,0:T(2,128)S(1)}, f32[2,128]{1,0:T(2,128)}, u32[]{:S(2)}) copy-start(f32[2,128]{1,0:T(2,128)} %param.4) | copy-start | bytes 3076
  0.6 51.3 %copy-start.4 = (f32[128]{0:T(128)S(1)}, f32[128]{0:T(128)}, u32[]{:S(2)}) copy-start(f32[128]{0:T(128)} %param.5) | copy-start | bytes 1540
  2.2 9.0 %collective-permute-start = (f32[67,128]{1,0:T(8,128)S(1)}, f32[67,128]{1,0:T(8,128)S(1)}, u32[]{:S(2)}, u32[]{:S(2)}) collective-permute-start(f32[67,128]{1,0:T(8,128)S(1)} %get-tuple-element.18), channel_id=1, source_target_pairs={{0,1},{1,2},{2,3},{3,4},{4,5},{5,6},{6,7},{7,8},{8,9},{9,10},{10,1... | collective-permute-start | bytes 102920 | tf_op jit(solution)/shard_map/ppermute | solution.py:25
  12.0 6.2 %collective-permute-start.1 = (f32[67,256]{1,0:T(8,128)S(1)}, f32[67,256]{1,0:T(8,128)S(1)}, u32[]{:S(2)}, u32[]{:S(2)}) collective-permute-start(f32[67,256]{1,0:T(8,128)S(1)} %pad_maximum_fusion.2), channel_id=1, source_target_pairs={{0,2},{1,3},{2,4},{3,5},{4,6},{5,7},{6,8},{7,9},{8,10},{9,11},{10,... | collective-permute-start | bytes 205832 | tf_op jit(solution)/shard_map/ppermute | solution.py:25
  19.0 5.3 %collective-permute-start.2 = (f32[67,512]{1,0:T(8,128)S(1)}, f32[67,512]{1,0:T(8,128)S(1)}, u32[]{:S(2)}, u32[]{:S(2)}) collective-permute-start(f32[67,512]{1,0:T(8,128)S(1)} %pad_maximum_fusion.1), channel_id=1, source_target_pairs={{0,4},{1,5},{2,6},{3,7},{4,8},{5,9},{6,10},{7,11},{8,12},{9,13},{1... | collective-permute-start | bytes 411656 | tf_op jit(solution)/shard_map/ppermute | solution.py:25
  25.1 7.2 %collective-permute-start.3 = (f32[67,1024]{1,0:T(8,128)S(1)}, f32[67,1024]{1,0:T(8,128)S(1)}, u32[]{:S(2)}, u32[]{:S(2)}) collective-permute-start(f32[67,1024]{1,0:T(8,128)S(1)} %pad_maximum_fusion), channel_id=1, source_target_pairs={{0,8},{1,9},{2,10},{3,11},{4,12},{5,13},{6,14},{7,15},{8,0},{9,1},... | collective-permute-start | bytes 823304 | tf_op jit(solution)/shard_map/ppermute | solution.py:25
  37.1 253.6 %all-to-all-start = ((f32[16,67,2048]{2,1,0:T(8,128)}), f32[16,67,2048]{2,1,0:T(8,128)}, u32[]{:S(2)}, u32[]{:S(2)}) async-start(f32[16,67,2048]{2,1,0:T(8,128)} %stack.16), calls=%async_computation | async-start | bytes 18874368 | tf_op jit(solution)/shard_map/all_to_all | solution.py:32
  293.1 5.1 %copy-start.1 = (f32[64,128]{1,0:T(8,128)S(1)}, f32[64,128]{1,0:T(8,128)}, u32[]{:S(2)}) copy-start(f32[64,128]{1,0:T(8,128)} %param.3) | copy-start | bytes 98308
  337.5 24.4 %copy-start = (f32[128,32768]{0,1:T(8,128)}, f32[128,32768]{0,1:T(8,128)S(1)}, u32[]{:S(2)}) copy-start(f32[128,32768]{0,1:T(8,128)S(1)} %get-tuple-element.25) | copy-start | bytes 50331652
  344.1 107.8 %copy-start.3 = (f32[128]{0:T(128)}, f32[128]{0:T(128)S(1)}, u32[]{:S(2)}) copy-start(f32[128]{0:T(128)S(1)} %get-tuple-element.10) | copy-start | bytes 1540
  362.6 6.4 %collective-permute-start.4 = (f32[4,128]{1,0:T(4,128)S(1)}, f32[4,128]{1,0:T(4,128)S(1)}, u32[]{:S(2)}, u32[]{:S(2)}) collective-permute-start(f32[4,128]{1,0:T(4,128)S(1)} %get-tuple-element.20), channel_id=1, source_target_pairs={{0,1},{1,2},{2,3},{3,4},{4,5},{5,6},{6,7},{7,8},{8,9},{9,10},{10,1... | collective-permute-start | bytes 6152 | tf_op jit(solution)/shard_map/ppermute | solution.py:25
  369.0 5.5 %collective-permute-start.5 = (f32[4,256]{1,0:T(4,128)S(1)}, f32[4,256]{1,0:T(4,128)S(1)}, u32[]{:S(2)}, u32[]{:S(2)}) collective-permute-start(f32[4,256]{1,0:T(4,128)S(1)} %pad_maximum_fusion.6), channel_id=1, source_target_pairs={{0,2},{1,3},{2,4},{3,5},{4,6},{5,7},{6,8},{7,9},{8,10},{9,11},{10,... | collective-permute-start | bytes 12296 | tf_op jit(solution)/shard_map/ppermute | solution.py:25
  374.5 11.6 %collective-permute-start.6 = (f32[4,512]{1,0:T(4,128)S(1)}, f32[4,512]{1,0:T(4,128)S(1)}, u32[]{:S(2)}, u32[]{:S(2)}) collective-permute-start(f32[4,512]{1,0:T(4,128)S(1)} %pad_maximum_fusion.5), channel_id=1, source_target_pairs={{0,4},{1,5},{2,6},{3,7},{4,8},{5,9},{6,10},{7,11},{8,12},{9,13},{1... | collective-permute-start | bytes 24584 | tf_op jit(solution)/shard_map/ppermute | solution.py:25
  386.2 4.2 collective-permute-start.7
  391.2 33.3 %all-to-all-start.1 = ((f32[16,4,2048]{2,1,0:T(4,128)}), f32[16,4,2048]{2,1,0:T(4,128)S(1)}, u32[]{:S(2)}, u32[]{:S(2)}) async-start(f32[16,4,2048]{2,1,0:T(4,128)} %stack.20), calls=%async_computation.1 | async-start | bytes 1048576 | tf_op jit(solution)/shard_map/all_to_all | solution.py:32
